TPU v7x, 256 devices: a whole 4x4x8 slice. The times are simulated.
256 devices in a mesh: gx: 8 (over x, core), gy: 8 (over z), gz: 4 (over y).
Axes of the slice: x: 4, y: 4, z: 8, core: 2. Of those that a mesh axis runs over, the one named last changes fastest.
Arguments:
- orbitals: float32 [32, 64, 128, 512], P(None, 'gx', 'gy', 'gz'), may hold values from -12 to 12
- potential: float32 [64, 128, 512], P('gx', 'gy', 'gz'), may hold values from -1 to 1
Outputs:
- filtered_basis: float32 [32, 64, 128, 512], P(None, 'gx', 'gy', 'gz')
- r_factor: float32 [32, 32], replicated
All inputs are finite; a program needn't handle non-finite values.
Results may differ from a plain program's by a relative error of at most 0.00013.
Values sent between devices are 32-bit elements; how exact they have to be, the bound alone decides.
No kernel may reach another device: no remote copies, remote signals or barrier semaphores. Data moves between devices by JAX's collectives and lax.ppermute only.
A program may use at most 128 MiB of HBM per device.

v0:
```python
import jax
import jax.numpy as jnp
from jax import lax
from jax.sharding import PartitionSpec as P

TAPS = (-1.0 / 12.0, 4.0 / 3.0, -2.5, 4.0 / 3.0, -1.0 / 12.0)


def padded_2(x, sides, width):
    for axis, dim in sides:
        devices, length = (lax.axis_size(axis), x.shape[dim])
        up = [(i, (i + 1) % devices) for i in range(devices)]
        down = [(j, i) for i, j in up]
        last = lax.slice_in_dim(x, length - width, length, axis=dim)
        leading = lax.slice_in_dim(x, 0, width, axis=dim)
        before = lax.ppermute(last, axis, up)
        after = lax.ppermute(leading, axis, down)
        x = jnp.concatenate([before, x, after], axis=dim)
    return x


def window(padded, shift_x, shift_y, shift_z):
    sizes = padded.shape
    return padded[
        :,
        2 + shift_x : sizes[1] - 2 + shift_x,
        2 + shift_y : sizes[2] - 2 + shift_y,
        2 + shift_z : sizes[3] - 2 + shift_z,
    ]


def laplacian(padded):
    summed = 3.0 * TAPS[2] * window(padded, 0, 0, 0)
    for offset, weight in ((-2, TAPS[0]), (-1, TAPS[1]), (1, TAPS[3]), (2, TAPS[4])):
        summed = summed + weight * window(padded, offset, 0, 0)
        summed = summed + weight * window(padded, 0, offset, 0)
        summed = summed + weight * window(padded, 0, 0, offset)
    return summed


def hamiltonian(padded, potential_core):
    return -0.5 * laplacian(padded) + potential_core * window(padded, 0, 0, 0)


def with_rims(field):
    return padded_2(field, (("gx", 1), ("gy", 2), ("gz", 3)), 2)


def per_device(orbitals, potential):
    potential_cube = potential[None]
    first = (hamiltonian(with_rims(orbitals), potential_cube) - 5.5 * orbitals) / 3.5
    second = 2.0 * (hamiltonian(with_rims(first), potential_cube) - 5.5 * first) / 3.5 - orbitals
    norb_count = orbitals.shape[0]
    filtered = second.reshape(norb_count, -1)
    all_cells = filtered.shape[1] * lax.axis_size("gx") * lax.axis_size("gy") * lax.axis_size("gz")
    correlation = jnp.dot(filtered, filtered.T, precision=lax.Precision.HIGHEST) / all_cells
    lower = jnp.linalg.cholesky(lax.psum(correlation, ("gx", "gy", "gz")))
    basis = jax.scipy.linalg.solve_triangular(lower, filtered, lower=True)
    return (basis.reshape(orbitals.shape), lower.T)


def solution(mesh):
    in_specs = (P(None, "gx", "gy", "gz"), P("gx", "gy", "gz"))
    out_specs = (P(None, "gx", "gy", "gz"), P())
    return jax.shard_map(
        per_device, mesh=mesh, in_specs=in_specs, out_specs=out_specs, check_vma=False
    )
```

profile of v0, /device:TPU:1, one launch (start us, length us, event | category | flops | bytes accessed | tf_op | source)
XLA Modules:
  0.0 230.9 jit_solution(3430019254784717829)
XLA Ops:
  2.2 2.6 %collective-permute-start = (f32[32,2,16,128]{3,0,2,1:T(8,128)S(1)}, f32[32,2,16,128]{3,0,2,1:T(8,128)S(1)}, u32[]{:S(2)}, u32[]{:S(2)}) collective-permute-start(f32[32,2,16,128]{3,0,2,1:T(8,128)S(1)} %copy.80), channel_id=1, source_target_pairs={{0,32},{32,64},{64,96},{96,128},{128,160},{160,192},{192,224},{224... | collective-permute-start | bytes 1572872 | tf_op jit(solution)/shard_map/ppermute | solution.py:16
  5.8 5.2 %collective-permute-done = f32[32,2,16,128]{3,0,2,1:T(8,128)S(1)} collective-permute-done((f32[32,2,16,128]{3,0,2,1:T(8,128)S(1)}, f32[32,2,16,128]{3,0,2,1:T(8,128)S(1)}, u32[]{:S(2)}, u32[]{:S(2)}) %collective-permute-start) | collective-permute-done | bytes 524320 | tf_op jit(solution)/shard_map/ppermute | solution.py:16
  15.6 4.0 %collective-permute-start.3 = (f32[32,12,2,128]{3,0,2,1:T(8,128)S(1)}, f32[32,12,2,128]{3,0,2,1:T(8,128)S(1)}, u32[]{:S(2)}, u32[]{:S(2)}) collective-permute-start(f32[32,12,2,128]{3,0,2,1:T(8,128)S(1)} %get-tuple-element.21), channel_id=1, source_target_pairs={{4,0},{8,4},{12,8},{16,12},{20,16},{24,20},{28,24},{0,28},{5,1},{9... | collective-permute-start | bytes 1179656 | tf_op jit(solution)/shard_map/ppermute | solution.py:17
  19.7 8.1 %collective-permute-done.2 = f32[32,12,2,128]{3,0,2,1:T(8,128)S(1)} collective-permute-done((f32[32,12,2,128]{3,0,2,1:T(8,128)S(1)}, f32[32,12,2,128]{3,0,2,1:T(8,128)S(1)}, u32[]{:S(2)}, u32[]{:S(2)}) %collective-permute-start.2) | collective-permute-done | bytes 393248 | tf_op jit(solution)/shard_map/ppermute | solution.py:16
  28.2 4.7 %fusion.56 = (f32[32,12,20,2]{3,0,2,1:T(8,128)}, f32[32,12,20,2]{3,0,2,1:T(8,128)}) fusion(f32[32,12,20,128]{3,0,2,1:T(8,128)S(1)} %pad_maximum_fusion), kind=kLoop, calls=%fused_computation.120 | loop fusion | bytes 245760 | tf_op jit(solution)/shard_map/slice | solution.py:14
  32.9 3.4 %copy.47 = f32[32,12,20,2]{0,2,3,1:T(8,128)S(1)} copy(f32[32,12,20,2]{3,0,2,1:T(8,128)} %get-tuple-element.14) | data formatting | bytes 122880 | tf_op jit(solution)/shard_map/slice | solution.py:14
  37.6 3.4 %copy.50 = f32[32,12,20,2]{0,2,3,1:T(8,128)S(1)} copy(f32[32,12,20,2]{3,0,2,1:T(8,128)} %get-tuple-element.15) | data formatting | bytes 122880 | tf_op jit(solution)/shard_map/slice | solution.py:15
  41.0 1.7 collective-permute-start.5
  42.7 1.6 collective-permute-done.4
  44.3 2.9 %copy.48 = f32[32,12,20,2]{3,0,2,1:T(8,128)} copy(f32[32,12,20,2]{0,2,3,1:T(8,128)S(1)} %collective-permute-done.4) | data formatting | bytes 122880 | tf_op jit(solution)/shard_map/ppermute | solution.py:16
  47.7 2.9 %copy.51 = f32[32,12,20,2]{3,0,2,1:T(8,128)} copy(f32[32,12,20,2]{0,2,3,1:T(8,128)S(1)} %collective-permute-done.5) | data formatting | bytes 122880 | tf_op jit(solution)/shard_map/ppermute | solution.py:17
  50.5 17.0 %broadcast_multiply_fusion = (f32[32,8,16,128]{3,0,2,1:T(8,128)S(1)}, f32[32,8,16,128]{3,0,2,1:T(8,128)}) fusion(f32[8,16,128]{2,1,0:T(8,128)S(1)} %copy-done.5, f32[32,12,20,2]{3,0,2,1:T(8,128)} %copy.51, f32[32,12,2,128]{3,0,2,1:T(8,128)S(1)} %collective-permute-done.3, f32[32,12,16,128]{3,0,2,1:T(8,128)} %copy-done.1, ...), kind=kLoop, calls=%fused_computation.97 | loop fusion | flops 24641536 | bytes 18800640 | tf_op jit(solution)/shard_map/div | solution.py:51
  67.6 5.3 %collective-permute-start.6 = (f32[32,2,16,128]{3,0,2,1:T(8,128)S(1)}, f32[32,2,16,128]{3,0,2,1:T(8,128)S(1)}, u32[]{:S(2)}, u32[]{:S(2)}) collective-permute-start(f32[32,2,16,128]{3,0,2,1:T(8,128)S(1)} %get-tuple-element.22), channel_id=1, source_target_pairs={{0,32},{32,64},{64,96},{96,128},{128,160},{160,192},{192,224},{224... | collective-permute-start | bytes 1572872 | tf_op jit(solution)/shard_map/ppermute | solution.py:16
  72.9 6.1 %collective-permute-done.6 = f32[32,2,16,128]{3,0,2,1:T(8,128)S(1)} collective-permute-done((f32[32,2,16,128]{3,0,2,1:T(8,128)S(1)}, f32[32,2,16,128]{3,0,2,1:T(8,128)S(1)}, u32[]{:S(2)}, u32[]{:S(2)}) %collective-permute-start.6) | collective-permute-done | bytes 524320 | tf_op jit(solution)/shard_map/ppermute | solution.py:16
  79.1 2.5 %collective-permute-done.7 = f32[32,2,16,128]{3,0,2,1:T(8,128)S(1)} collective-permute-done((f32[32,2,16,128]{3,0,2,1:T(8,128)S(1)}, f32[32,2,16,128]{3,0,2,1:T(8,128)S(1)}, u32[]{:S(2)}, u32[]{:S(2)}) %collective-permute-start.7) | collective-permute-done | bytes 524320 | tf_op jit(solution)/shard_map/ppermute | solution.py:17
  81.7 2.7 %collective-permute-start.9 = (f32[32,12,2,128]{3,0,2,1:T(8,128)S(1)}, f32[32,12,2,128]{3,0,2,1:T(8,128)S(1)}, u32[]{:S(2)}, u32[]{:S(2)}) collective-permute-start(f32[32,12,2,128]{3,0,2,1:T(8,128)S(1)} %get-tuple-element.19), channel_id=1, source_target_pairs={{4,0},{8,4},{12,8},{16,12},{20,16},{24,20},{28,24},{0,28},{5,1},{9... | collective-permute-start | bytes 1179656 | tf_op jit(solution)/shard_map/ppermute | solution.py:17
  85.0 8.1 %collective-permute-done.8 = f32[32,12,2,128]{3,0,2,1:T(8,128)S(1)} collective-permute-done((f32[32,12,2,128]{3,0,2,1:T(8,128)S(1)}, f32[32,12,2,128]{3,0,2,1:T(8,128)S(1)}, u32[]{:S(2)}, u32[]{:S(2)}) %collective-permute-start.8) | collective-permute-done | bytes 393248 | tf_op jit(solution)/shard_map/ppermute | solution.py:16
  94.0 4.7 %fusion.55 = (f32[32,12,20,2]{3,0,2,1:T(8,128)}, f32[32,12,20,2]{3,0,2,1:T(8,128)}) fusion(f32[32,12,20,128]{3,0,2,1:T(8,128)S(1)} %pad_maximum_fusion.1), kind=kLoop, calls=%fused_computation.119 | loop fusion | bytes 245760 | tf_op jit(solution)/shard_map/slice | solution.py:14
  98.6 4.0 %copy.54 = f32[32,12,20,2]{0,2,3,1:T(8,128)} copy(f32[32,12,20,2]{3,0,2,1:T(8,128)} %get-tuple-element.12) | data formatting | bytes 122880 | tf_op jit(solution)/shard_map/slice | solution.py:14
  102.7 4.0 %copy.56 = f32[32,12,20,2]{0,2,3,1:T(8,128)} copy(f32[32,12,20,2]{3,0,2,1:T(8,128)} %get-tuple-element.13) | data formatting | bytes 122880 | tf_op jit(solution)/shard_map/slice | solution.py:15
  106.7 2.7 %collective-permute-start.11 = (f32[32,12,20,2]{0,2,3,1:T(8,128)}, f32[32,12,20,2]{0,2,3,1:T(8,128)}, u32[]{:S(2)}, u32[]{:S(2)}) collective-permute-start(f32[32,12,20,2]{0,2,3,1:T(8,128)} %copy.56), channel_id=1, source_target_pairs={{1,0},{2,1},{3,2},{0,3},{5,4},{6,5},{7,6},{4,7},{9,8},{10,9},{11,1... | collective-permute-start | bytes 184328 | tf_op jit(solution)/shard_map/ppermute | solution.py:17
  109.4 4.3 %maximum_maximum_fusion = (f32[32,12,18,128]{3,0,2,1:T(8,128)}, f32[32,12,18,128]{3,0,2,1:T(8,128)}) fusion(f32[32,2,16,128]{3,0,2,1:T(8,128)S(1)} %collective-permute-done.7, f32[32,8,16,128]{3,0,2,1:T(8,128)S(1)} %get-tuple-element.10, f32[32,2,16,128]{3,0,2,1:T(8,128)S(1)} %collective-permute-done.6, f32[32,12,2,128]{3,0,2,1:T(8,128)S(1)} %collective-permute-done.8, ...), kind=kLoop, calls=%fused_computation.6 | loop fusion | flops 5308416 | bytes 11010048 | tf_op jit(solution)/shard_map/concatenate | solution.py:18
  113.7 5.4 %collective-permute-done.10 = f32[32,12,20,2]{0,2,3,1:T(8,128)} collective-permute-done((f32[32,12,20,2]{0,2,3,1:T(8,128)}, f32[32,12,20,2]{0,2,3,1:T(8,128)}, u32[]{:S(2)}, u32[]{:S(2)}) %collective-permute-start.10) | collective-permute-done | bytes 61472 | tf_op jit(solution)/shard_map/ppermute | solution.py:16
  119.1 3.7 %copy.55 = f32[32,12,20,2]{3,0,2,1:T(8,128)} copy(f32[32,12,20,2]{0,2,3,1:T(8,128)} %collective-permute-done.10) | data formatting | bytes 122880 | tf_op jit(solution)/shard_map/ppermute | solution.py:16
  122.9 3.8 %copy.57 = f32[32,12,20,2]{3,0,2,1:T(8,128)} copy(f32[32,12,20,2]{0,2,3,1:T(8,128)} %collective-permute-done.11) | data formatting | bytes 122880 | tf_op jit(solution)/shard_map/ppermute | solution.py:17
  126.6 9.9 %fusion.12 = f32[32,8,16,128]{3,0,2,1:T(8,128)S(1)} fusion(f32[32,8,16,128]{3,0,2,1:T(8,128)S(1)} %get-tuple-element.10, f32[32,2,16,128]{3,0,2,1:T(8,128)S(1)} %collective-permute-done.7, f32[32,2,16,128]{3,0,2,1:T(8,128)S(1)} %collective-permute-done.6, f32[32,12,20,2]{3,0,2,1:T(8,128)} %copy.57, f32[32,12,2,128]{3,0,2,1:T(8,128)} %copy-done.4, ...), kind=kLoop, calls=%fused_computation.24 | loop fusion | flops 29360128 | bytes 18800640 | tf_op jit(solution)/shard_map/sub | solution.py:52
  136.5 1.8 fusion.50
  139.5 76.7 %psum.7 = f32[32,32]{0,1:T(8,128)S(1)} all-reduce(f32[32,32]{0,1:T(8,128)S(1)} %fusion.50), channel_id=1, replica_groups=mesh['gx'=8,'gy'=8,'gz'=4] {'gx','gy','gz'}, use_global_device_ids=true, to_apply=%region_0.0 | all-reduce | flops 1024 | bytes 8192 | tf_op jit(solution)/shard_map/psum | solution.py:57
  217.9 2.9 %cholesky.16 = f32[32,32]{1,0:T(8,128)S(1)} custom-call(f32[32,32]{1,0:T(8,128)S(1)} %fusion.52), custom_call_target="Cholesky" | custom-call | tf_op jit(solution)/shard_map/jit(cholesky)/cholesky | solution.py:57
  222.8 2.4 %custom-call.7 = f32[1,32,32]{1,2,0:T(8,128)S(1)} custom-call(f32[1,32,32]{2,1,0:T(8,128)S(1)} %get-tuple-element.34), custom_call_target="InvertDiagBlocksLowerTriangular" | custom-call | tf_op jit(solution)/shard_map/jit(_solve_triangular)/triangular_solve | solution.py:58
  225.3 3.0 %fusion.48 = f32[32,8,16,128]{3,0,2,1:T(8,128)S(1)} fusion(f32[8,16,128,32]{2,1,0,3:T(8,128)S(1)} %bitcast.32, f32[1,32,32]{1,2,0:T(8,128)S(1)} %custom-call.7), kind=kOutput, calls=%fused_computation.93 | convolution fusion | flops 201326592 | bytes 4198400 | tf_op jit(solution)/shard_map/jit(_solve_triangular)/triangular_solve | solution.py:58
  228.3 2.5 %copy.64 = f32[32,8,16,128]{3,2,1,0:T(8,128)} copy(f32[32,8,16,128]{3,0,2,1:T(8,128)S(1)} %fusion.48) | data formatting | bytes 4194304
  (46 shorter events, 16.0 us)
Async XLA Ops:
  1.9 9.2 %copy-start = (f32[32,8,16,128]{3,2,1,0:T(8,128)S(1)}, f32[32,8,16,128]{3,2,1,0:T(8,128)}, u32[]{:S(2)}) copy-start(f32[32,8,16,128]{3,2,1,0:T(8,128)} %param.2) | copy-start | bytes 6291460
  2.2 8.7 %collective-permute-start = (f32[32,2,16,128]{3,0,2,1:T(8,128)S(1)}, f32[32,2,16,128]{3,0,2,1:T(8,128)S(1)}, u32[]{:S(2)}, u32[]{:S(2)}) collective-permute-start(f32[32,2,16,128]{3,0,2,1:T(8,128)S(1)} %copy.80), channel_id=1, source_target_pairs={{0,32},{32,64},{64,96},{96,128},{128,160},{160,192},{192,224},{224... | collective-permute-start | bytes 1572872 | tf_op jit(solution)/shard_map/ppermute | solution.py:16
  5.1 8.9 %collective-permute-start.1 = (f32[32,2,16,128]{3,0,2,1:T(8,128)S(1)}, f32[32,2,16,128]{3,0,2,1:T(8,128)S(1)}, u32[]{:S(2)}, u32[]{:S(2)}) collective-permute-start(f32[32,2,16,128]{3,0,2,1:T(8,128)S(1)} %copy.81), channel_id=1, source_target_pairs={{32,0},{64,32},{96,64},{128,96},{160,128},{192,160},{224,192},{0,2... | collective-permute-start | bytes 1572872 | tf_op jit(solution)/shard_map/ppermute | solution.py:17
  12.5 15.3 %copy-start.3 = (f32[32,10,16,128]{3,0,2,1:T(8,128)}, f32[32,10,16,128]{3,0,2,1:T(8,128)S(1)}, u32[]{:S(2)}) copy-start(f32[32,10,16,128]{3,0,2,1:T(8,128)S(1)} %get-tuple-element.24) | copy-start | bytes 7864324
  14.1 13.6 %copy-start.2 = (f32[32,10,16,128]{3,0,2,1:T(8,128)}, f32[32,10,16,128]{3,0,2,1:T(8,128)S(1)}, u32[]{:S(2)}) copy-start(f32[32,10,16,128]{3,0,2,1:T(8,128)S(1)} %get-tuple-element.31) | copy-start | bytes 7864324
  14.2 13.6 %copy-start.1 = (f32[32,12,16,128]{3,0,2,1:T(8,128)}, f32[32,12,16,128]{3,0,2,1:T(8,128)S(1)}, u32[]{:S(2)}) copy-start(f32[32,12,16,128]{3,0,2,1:T(8,128)S(1)} %get-tuple-element.32) | copy-start | bytes 9437188
  14.2 13.5 %collective-permute-start.2 = (f32[32,12,2,128]{3,0,2,1:T(8,128)S(1)}, f32[32,12,2,128]{3,0,2,1:T(8,128)S(1)}, u32[]{:S(2)}, u32[]{:S(2)}) collective-permute-start(f32[32,12,2,128]{3,0,2,1:T(8,128)S(1)} %get-tuple-element.20), channel_id=1, source_target_pairs={{0,4},{4,8},{8,12},{12,16},{16,20},{20,24},{24,28},{28,0},{1,5},{5... | collective-permute-start | bytes 1179656 | tf_op jit(solution)/shard_map/ppermute | solution.py:16
  15.6 12.1 %collective-permute-start.3 = (f32[32,12,2,128]{3,0,2,1:T(8,128)S(1)}, f32[32,12,2,128]{3,0,2,1:T(8,128)S(1)}, u32[]{:S(2)}, u32[]{:S(2)}) collective-permute-start(f32[32,12,2,128]{3,0,2,1:T(8,128)S(1)} %get-tuple-element.21), channel_id=1, source_target_pairs={{4,0},{8,4},{12,8},{16,12},{20,16},{24,20},{28,24},{0,28},{5,1},{9... | collective-permute-start | bytes 1179656 | tf_op jit(solution)/shard_map/ppermute | solution.py:17
  36.3 8.1 %collective-permute-start.4 = (f32[32,12,20,2]{0,2,3,1:T(8,128)S(1)}, f32[32,12,20,2]{0,2,3,1:T(8,128)S(1)}, u32[]{:S(2)}, u32[]{:S(2)}) collective-permute-start(f32[32,12,20,2]{0,2,3,1:T(8,128)S(1)} %copy.47), channel_id=1, source_target_pairs={{0,1},{1,2},{2,3},{3,0},{4,5},{5,6},{6,7},{7,4},{8,9},{9,10},{10,1... | collective-permute-start | bytes 184328 | tf_op jit(solution)/shard_map/ppermute | solution.py:16
  41.0 6.7 %collective-permute-start.5 = (f32[32,12,20,2]{0,2,3,1:T(8,128)S(1)}, f32[32,12,20,2]{0,2,3,1:T(8,128)S(1)}, u32[]{:S(2)}, u32[]{:S(2)}) collective-permute-start(f32[32,12,20,2]{0,2,3,1:T(8,128)S(1)} %copy.50), channel_id=1, source_target_pairs={{1,0},{2,1},{3,2},{0,3},{5,4},{6,5},{7,6},{4,7},{9,8},{10,9},{11,1... | collective-permute-start | bytes 184328 | tf_op jit(solution)/shard_map/ppermute | solution.py:17
  47.2 3.3 %copy-start.5 = (f32[8,16,128]{2,1,0:T(8,128)S(1)}, f32[8,16,128]{2,1,0:T(8,128)}, u32[]{:S(2)}) copy-start(f32[8,16,128]{2,1,0:T(8,128)} %param.3) | copy-start | bytes 196612
  67.6 16.8 %copy-start.6 = (f32[8,16,128]{2,1,0:T(8,128)S(1)}, f32[8,16,128]{2,1,0:T(8,128)}, u32[]{:S(2)}) copy-start(f32[8,16,128]{2,1,0:T(8,128)} %param.3) | copy-start | bytes 196612
  67.6 11.5 %collective-permute-start.6 = (f32[32,2,16,128]{3,0,2,1:T(8,128)S(1)}, f32[32,2,16,128]{3,0,2,1:T(8,128)S(1)}, u32[]{:S(2)}, u32[]{:S(2)}) collective-permute-start(f32[32,2,16,128]{3,0,2,1:T(8,128)S(1)} %get-tuple-element.22), channel_id=1, source_target_pairs={{0,32},{32,64},{64,96},{96,128},{128,160},{160,192},{192,224},{224... | collective-permute-start | bytes 1572872 | tf_op jit(solution)/shard_map/ppermute | solution.py:16
  72.9 8.6 %collective-permute-start.7 = (f32[32,2,16,128]{3,0,2,1:T(8,128)S(1)}, f32[32,2,16,128]{3,0,2,1:T(8,128)S(1)}, u32[]{:S(2)}, u32[]{:S(2)}) collective-permute-start(f32[32,2,16,128]{3,0,2,1:T(8,128)S(1)} %get-tuple-element.23), channel_id=1, source_target_pairs={{32,0},{64,32},{96,64},{128,96},{160,128},{192,160},{224,192},{0,2... | collective-permute-start | bytes 1572872 | tf_op jit(solution)/shard_map/ppermute | solution.py:17
  81.6 11.5 %collective-permute-start.8 = (f32[32,12,2,128]{3,0,2,1:T(8,128)S(1)}, f32[32,12,2,128]{3,0,2,1:T(8,128)S(1)}, u32[]{:S(2)}, u32[]{:S(2)}) collective-permute-start(f32[32,12,2,128]{3,0,2,1:T(8,128)S(1)} %get-tuple-element.18), channel_id=1, source_target_pairs={{0,4},{4,8},{8,12},{12,16},{16,20},{20,24},{24,28},{28,0},{1,5},{5... | collective-permute-start | bytes 1179656 | tf_op jit(solution)/shard_map/ppermute | solution.py:16
  81.7 11.4 %collective-permute-start.9 = (f32[32,12,2,128]{3,0,2,1:T(8,128)S(1)}, f32[32,12,2,128]{3,0,2,1:T(8,128)S(1)}, u32[]{:S(2)}, u32[]{:S(2)}) collective-permute-start(f32[32,12,2,128]{3,0,2,1:T(8,128)S(1)} %get-tuple-element.19), channel_id=1, source_target_pairs={{4,0},{8,4},{12,8},{16,12},{20,16},{24,20},{28,24},{0,28},{5,1},{9... | collective-permute-start | bytes 1179656 | tf_op jit(solution)/shard_map/ppermute | solution.py:17
  93.1 0.9 copy-start.4
  106.7 16.2 %collective-permute-start.11 = (f32[32,12,20,2]{0,2,3,1:T(8,128)}, f32[32,12,20,2]{0,2,3,1:T(8,128)}, u32[]{:S(2)}, u32[]{:S(2)}) collective-permute-start(f32[32,12,20,2]{0,2,3,1:T(8,128)} %copy.56), channel_id=1, source_target_pairs={{1,0},{2,1},{3,2},{0,3},{5,4},{6,5},{7,6},{4,7},{9,8},{10,9},{11,1... | collective-permute-start | bytes 184328 | tf_op jit(solution)/shard_map/ppermute | solution.py:17
  109.4 9.8 %collective-permute-start.10 = (f32[32,12,20,2]{0,2,3,1:T(8,128)}, f32[32,12,20,2]{0,2,3,1:T(8,128)}, u32[]{:S(2)}, u32[]{:S(2)}) collective-permute-start(f32[32,12,20,2]{0,2,3,1:T(8,128)} %copy.54), channel_id=1, source_target_pairs={{0,1},{1,2},{2,3},{3,0},{4,5},{5,6},{6,7},{7,4},{8,9},{9,10},{10,1... | collective-permute-start | bytes 184328 | tf_op jit(solution)/shard_map/ppermute | solution.py:16
where the time goes:
time: 231 us
  blocking collectives  76.7 us (33%)
  local copies, waits for them, and re-layouts  47.5 us (21%)
  other arithmetic  39.4 us (17%)
  waiting for transfers between devices  39.1 us (17%)
  starting transfers between devices  22.5 us (10%)
  matrix products  4.81 us (2%)
    psum x1, blocking collectives, per_device(): lower = jnp.linalg.cholesky(lax.psum(correlation, ('gx', 'gy', 'gz')))  76.7 us
    ppermute x6, waiting for transfers between devices, padded_2(): before = lax.ppermute(last, axis, up)  34.6 us
    div x1, other arithmetic, per_device(): (hamiltonian(with_rims(orbitals), potential_cube) - 5.5 * orbitals) / 3.5  17 us
    slice x6, local copies, waits for them, and re-layouts, padded_2(): last = lax.slice_in_dim(x, length - width, length, axis=dim)  16.9 us
    ppermute x6, starting transfers between devices, padded_2(): after = lax.ppermute(leading, axis, down)  11.7 us
    ppermute x6, starting transfers between devices, padded_2(): before = lax.ppermute(last, axis, up)  10.8 us
    sub x1, other arithmetic, per_device(): 2.0 * (hamiltonian(with_rims(first), potential_cube) - 5.5 * first) / 3.5  9.89 us
    slice x3, local copies, waits for them, and re-layouts, padded_2(): leading = lax.slice_in_dim(x, 0, width, axis=dim)  8.68 us
  transfers between devices with their start and end apart: 12, of which 9 were waited for; matrix products, arithmetic and copies ran while one was open for 7% of the time, Pallas kernels for 0%

commit v1 on v0

--- a/solution.py
+++ b/solution.py
@@ -4,6 +4,12 @@
 from jax.sharding import PartitionSpec as P
 
 TAPS = (-1.0 / 12.0, 4.0 / 3.0, -2.5, 4.0 / 3.0, -1.0 / 12.0)
+
+
+def summed_here(x, axis):
+    pieces = lax.all_gather(x, axis, axis=0, tiled=False)
+    acc = pieces.sum(axis=0)
+    return acc
 
 
 def padded_2(x, sides, width):
@@ -54,7 +60,7 @@
     filtered = second.reshape(norb_count, -1)
     all_cells = filtered.shape[1] * lax.axis_size("gx") * lax.axis_size("gy") * lax.axis_size("gz")
     correlation = jnp.dot(filtered, filtered.T, precision=lax.Precision.HIGHEST) / all_cells
-    lower = jnp.linalg.cholesky(lax.psum(correlation, ("gx", "gy", "gz")))
+    lower = jnp.linalg.cholesky(summed_here(correlation, ("gx", "gy", "gz")))
     basis = jax.scipy.linalg.solve_triangular(lower, filtered, lower=True)
     return (basis.reshape(orbitals.shape), lower.T)
 

time: 231 us -> 284 us (1.23)
  waiting for transfers between devices: 39.1 us -> 149 us
  blocking collectives: 76.7 us -> 0 us
  between operations: 0.85 us -> 14.2 us
  other arithmetic: 39.4 us -> 42.7 us
  local copies, waits for them, and re-layouts: 47.5 us -> 50.4 us
    all_gather x0 -> x1, waiting for transfers between devices: none -> 110 us  [summed_here(): pieces = lax.all_gather(x, axis, axis=0, tiled=False)]
    psum x1 -> x0, blocking collectives: 76.7 us -> none  [per_device(): lower = jnp.linalg.cholesky(lax.psum(correlation, ('gx', 'gy', 'gz')))]
    unnamed x21 -> x23, local copies, waits for them, and re-layouts: 6 us -> 7.3 us
  transfers between devices with their start and end apart: 12 -> 13, of which waited for: 9 -> 10; matrix products, arithmetic and copies ran while one was open for 7% -> 7% of each run, Pallas kernels for 0% -> 0%
where the time goes in v1:
time: 284 us
  waiting for transfers between devices  149 us (52%)
  local copies, waits for them, and re-layouts  50.4 us (18%)
  other arithmetic  42.7 us (15%)
  starting transfers between devices  22.6 us (8%)
  between operations  14.2 us (5%)
  matrix products  5.42 us (2%)
    all_gather x1, waiting for transfers between devices, summed_here(): pieces = lax.all_gather(x, axis, axis=0, tiled=False)  110 us
    ppermute x6, waiting for transfers between devices, padded_2(): before = lax.ppermute(last, axis, up)  34.5 us
    div x1, other arithmetic, per_device(): (hamiltonian(with_rims(orbitals), potential_cube) - 5.5 * orbitals) / 3.5  17.4 us
    slice x6, local copies, waits for them, and re-layouts, padded_2(): last = lax.slice_in_dim(x, length - width, length, axis=dim)  16.9 us
    ppermute x6, starting transfers between devices, padded_2(): after = lax.ppermute(leading, axis, down)  11.7 us
    ppermute x6, starting transfers between devices, padded_2(): before = lax.ppermute(last, axis, up)  10.8 us
    sub x1, other arithmetic, per_device(): 2.0 * (hamiltonian(with_rims(first), potential_cube) - 5.5 * first) / 3.5  10.3 us
    slice x3, local copies, waits for them, and re-layouts, padded_2(): leading = lax.slice_in_dim(x, 0, width, axis=dim)  8.68 us
  transfers between devices with their start and end apart: 13, of which 10 were waited for; matrix products, arithmetic and copies ran while one was open for 7% of the time, Pallas kernels for 0%

profile of v1, /device:TPU:1, one launch (start us, length us, event | category | flops | bytes accessed | tf_op | source)
XLA Modules:
  0.0 284.0 jit_solution(16003422079930115617)
XLA Ops:
  8.8 2.6 collective-permute-start
  12.4 5.2 %collective-permute-done = f32[32,2,16,128]{3,0,2,1:T(8,128)S(1)} collective-permute-done((f32[32,2,16,128]{3,0,2,1:T(8,128)S(1)}, f32[32,2,16,128]{3,0,2,1:T(8,128)S(1)}, u32[]{:S(2)}, u32[]{:S(2)}) %collective-permute-start) | collective-permute-done | bytes 524320 | tf_op jit(solution)/shard_map/ppermute | solution.py:22
  22.2 4.0 %collective-permute-start.3 = (f32[32,12,2,128]{3,0,2,1:T(8,128)S(1)}, f32[32,12,2,128]{3,0,2,1:T(8,128)S(1)}, u32[]{:S(2)}, u32[]{:S(2)}) collective-permute-start(f32[32,12,2,128]{3,0,2,1:T(8,128)S(1)} %get-tuple-element.21), channel_id=1, source_target_pairs={{4,0},{8,4},{12,8},{16,12},{20,16},{24,20},{28,24},{0,28},{5,1},{9... | collective-permute-start | bytes 1179656 | tf_op jit(solution)/shard_map/ppermute | solution.py:23
  26.3 8.1 %collective-permute-done.2 = f32[32,12,2,128]{3,0,2,1:T(8,128)S(1)} collective-permute-done((f32[32,12,2,128]{3,0,2,1:T(8,128)S(1)}, f32[32,12,2,128]{3,0,2,1:T(8,128)S(1)}, u32[]{:S(2)}, u32[]{:S(2)}) %collective-permute-start.2) | collective-permute-done | bytes 393248 | tf_op jit(solution)/shard_map/ppermute | solution.py:22
  34.8 4.7 %fusion.56 = (f32[32,12,20,2]{3,0,2,1:T(8,128)}, f32[32,12,20,2]{3,0,2,1:T(8,128)}) fusion(f32[32,12,20,128]{3,0,2,1:T(8,128)S(1)} %pad_maximum_fusion), kind=kLoop, calls=%fused_computation.120 | loop fusion | bytes 245760 | tf_op jit(solution)/shard_map/slice | solution.py:20
  39.5 3.4 %copy.44 = f32[32,12,20,2]{0,2,3,1:T(8,128)S(1)} copy(f32[32,12,20,2]{3,0,2,1:T(8,128)} %get-tuple-element.14) | data formatting | bytes 122880 | tf_op jit(solution)/shard_map/slice | solution.py:20
  44.2 3.4 %copy.47 = f32[32,12,20,2]{0,2,3,1:T(8,128)S(1)} copy(f32[32,12,20,2]{3,0,2,1:T(8,128)} %get-tuple-element.15) | data formatting | bytes 122880 | tf_op jit(solution)/shard_map/slice | solution.py:21
  50.9 2.9 %copy.45 = f32[32,12,20,2]{3,0,2,1:T(8,128)} copy(f32[32,12,20,2]{0,2,3,1:T(8,128)S(1)} %collective-permute-done.4) | data formatting | bytes 122880 | tf_op jit(solution)/shard_map/ppermute | solution.py:22
  54.2 2.9 %copy.48 = f32[32,12,20,2]{3,0,2,1:T(8,128)} copy(f32[32,12,20,2]{0,2,3,1:T(8,128)S(1)} %collective-permute-done.5) | data formatting | bytes 122880 | tf_op jit(solution)/shard_map/ppermute | solution.py:23
  57.1 17.4 %broadcast_multiply_fusion = (f32[32,8,16,128]{3,0,2,1:T(8,128)S(1)}, f32[32,8,16,128]{3,0,2,1:T(8,128)}) fusion(f32[8,16,128]{2,1,0:T(8,128)S(1)} %copy-done.6, f32[32,12,20,2]{3,0,2,1:T(8,128)} %copy.48, f32[32,12,2,128]{3,0,2,1:T(8,128)S(1)} %collective-permute-done.3, f32[32,12,16,128]{3,0,2,1:T(8,128)} %copy-done.2, ...), kind=kLoop, calls=%fused_computation.97 | loop fusion | flops 24641536 | bytes 18800640 | tf_op jit(solution)/shard_map/div | solution.py:57
  74.6 5.3 %collective-permute-start.6 = (f32[32,2,16,128]{3,0,2,1:T(8,128)S(1)}, f32[32,2,16,128]{3,0,2,1:T(8,128)S(1)}, u32[]{:S(2)}, u32[]{:S(2)}) collective-permute-start(f32[32,2,16,128]{3,0,2,1:T(8,128)S(1)} %get-tuple-element.22), channel_id=1, source_target_pairs={{0,32},{32,64},{64,96},{96,128},{128,160},{160,192},{192,224},{224... | collective-permute-start | bytes 1572872 | tf_op jit(solution)/shard_map/ppermute | solution.py:22
  79.9 6.1 %collective-permute-done.6 = f32[32,2,16,128]{3,0,2,1:T(8,128)S(1)} collective-permute-done((f32[32,2,16,128]{3,0,2,1:T(8,128)S(1)}, f32[32,2,16,128]{3,0,2,1:T(8,128)S(1)}, u32[]{:S(2)}, u32[]{:S(2)}) %collective-permute-start.6) | collective-permute-done | bytes 524320 | tf_op jit(solution)/shard_map/ppermute | solution.py:22
  86.1 2.5 collective-permute-done.7
  88.7 2.7 collective-permute-start.9
  92.0 8.1 %collective-permute-done.8 = f32[32,12,2,128]{3,0,2,1:T(8,128)S(1)} collective-permute-done((f32[32,12,2,128]{3,0,2,1:T(8,128)S(1)}, f32[32,12,2,128]{3,0,2,1:T(8,128)S(1)}, u32[]{:S(2)}, u32[]{:S(2)}) %collective-permute-start.8) | collective-permute-done | bytes 393248 | tf_op jit(solution)/shard_map/ppermute | solution.py:22
  100.9 4.7 %fusion.55 = (f32[32,12,20,2]{3,0,2,1:T(8,128)}, f32[32,12,20,2]{3,0,2,1:T(8,128)}) fusion(f32[32,12,20,128]{3,0,2,1:T(8,128)S(1)} %pad_maximum_fusion.1), kind=kLoop, calls=%fused_computation.119 | loop fusion | bytes 245760 | tf_op jit(solution)/shard_map/slice | solution.py:20
  105.6 4.0 %copy.51 = f32[32,12,20,2]{0,2,3,1:T(8,128)} copy(f32[32,12,20,2]{3,0,2,1:T(8,128)} %get-tuple-element.12) | data formatting | bytes 122880 | tf_op jit(solution)/shard_map/slice | solution.py:20
  109.6 4.0 %copy.53 = f32[32,12,20,2]{0,2,3,1:T(8,128)} copy(f32[32,12,20,2]{3,0,2,1:T(8,128)} %get-tuple-element.13) | data formatting | bytes 122880 | tf_op jit(solution)/shard_map/slice | solution.py:21
  113.7 2.7 collective-permute-start.11
  116.3 4.3 %maximum_maximum_fusion = (f32[32,12,18,128]{3,0,2,1:T(8,128)}, f32[32,12,18,128]{3,0,2,1:T(8,128)}) fusion(f32[32,2,16,128]{3,0,2,1:T(8,128)S(1)} %collective-permute-done.7, f32[32,8,16,128]{3,0,2,1:T(8,128)S(1)} %get-tuple-element.10, f32[32,2,16,128]{3,0,2,1:T(8,128)S(1)} %collective-permute-done.6, f32[32,12,2,128]{3,0,2,1:T(8,128)S(1)} %collective-permute-done.8, ...), kind=kLoop, calls=%fused_computation.6 | loop fusion | flops 5308416 | bytes 11010048 | tf_op jit(solution)/shard_map/concatenate | solution.py:24
  120.7 5.4 %collective-permute-done.10 = f32[32,12,20,2]{0,2,3,1:T(8,128)} collective-permute-done((f32[32,12,20,2]{0,2,3,1:T(8,128)}, f32[32,12,20,2]{0,2,3,1:T(8,128)}, u32[]{:S(2)}, u32[]{:S(2)}) %collective-permute-start.10) | collective-permute-done | bytes 61472 | tf_op jit(solution)/shard_map/ppermute | solution.py:22
  126.1 3.8 %copy.52 = f32[32,12,20,2]{3,0,2,1:T(8,128)} copy(f32[32,12,20,2]{0,2,3,1:T(8,128)} %collective-permute-done.10) | data formatting | bytes 122880 | tf_op jit(solution)/shard_map/ppermute | solution.py:22
  129.8 3.8 %copy.54 = f32[32,12,20,2]{3,0,2,1:T(8,128)} copy(f32[32,12,20,2]{0,2,3,1:T(8,128)} %collective-permute-done.11) | data formatting | bytes 122880 | tf_op jit(solution)/shard_map/ppermute | solution.py:23
  133.6 10.3 %fusion.12 = f32[32,8,16,128]{3,0,2,1:T(8,128)S(1)} fusion(f32[32,8,16,128]{3,0,2,1:T(8,128)S(1)} %get-tuple-element.10, f32[32,2,16,128]{3,0,2,1:T(8,128)S(1)} %collective-permute-done.7, f32[32,2,16,128]{3,0,2,1:T(8,128)S(1)} %collective-permute-done.6, f32[32,12,20,2]{3,0,2,1:T(8,128)} %copy.54, f32[32,12,2,128]{3,0,2,1:T(8,128)} %copy-done.5, ...), kind=kLoop, calls=%fused_computation.24 | loop fusion | flops 29360128 | bytes 18800640 | tf_op jit(solution)/shard_map/sub | solution.py:58
  145.2 2.4 fusion.50
  147.6 2.8 copy.57
  152.0 109.5 %all-gather.3.cloned.1.call-done = f32[8192,32]{1,0:T(8,128)} async-done(((f32[32,32]{1,0:T(8,128)}), f32[8192,32]{1,0:T(8,128)}) %all-gather.3.cloned.1.call-update) | async-done | bytes 1048592 | tf_op jit(solution)/shard_map/all_gather | solution.py:10
  261.6 2.5 reduce_sum.9
  264.2 2.9 %cholesky.16 = f32[32,32]{1,0:T(8,128)S(1)} custom-call(f32[32,32]{1,0:T(8,128)S(1)} %fusion.52), custom_call_target="Cholesky" | custom-call | tf_op jit(solution)/shard_map/jit(cholesky)/cholesky | solution.py:63
  269.1 2.4 custom-call.7
  271.5 3.0 %fusion.48 = f32[32,8,16,128]{3,0,2,1:T(8,128)S(1)} fusion(f32[8,16,128,32]{2,1,0,3:T(8,128)S(1)} %bitcast.35, f32[1,32,32]{1,2,0:T(8,128)S(1)} %custom-call.7), kind=kOutput, calls=%fused_computation.93 | convolution fusion | flops 201326592 | bytes 4198400 | tf_op jit(solution)/shard_map/jit(_solve_triangular)/triangular_solve | solution.py:64
  274.6 2.5 copy.60
  (51 shorter events, 19.5 us)
Async XLA Ops:
  7.2 254.4 %all-gather.3.cloned.1.call-start = ((), (), s32[]{:S(2)}) async-start(), calls=%async_computation | async-start | bytes 4210688 | tf_op jit(solution)/shard_map/all_gather | solution.py:10
  8.5 9.2 %copy-start.1 = (f32[32,8,16,128]{3,2,1,0:T(8,128)S(1)}, f32[32,8,16,128]{3,2,1,0:T(8,128)}, u32[]{:S(2)}) copy-start(f32[32,8,16,128]{3,2,1,0:T(8,128)} %param.2) | copy-start | bytes 6291460
  8.8 8.7 %collective-permute-start = (f32[32,2,16,128]{3,0,2,1:T(8,128)S(1)}, f32[32,2,16,128]{3,0,2,1:T(8,128)S(1)}, u32[]{:S(2)}, u32[]{:S(2)}) collective-permute-start(f32[32,2,16,128]{3,0,2,1:T(8,128)S(1)} %copy.75), channel_id=1, source_target_pairs={{0,32},{32,64},{64,96},{96,128},{128,160},{160,192},{192,224},{224... | collective-permute-start | bytes 1572872 | tf_op jit(solution)/shard_map/ppermute | solution.py:22
  11.7 8.9 %collective-permute-start.1 = (f32[32,2,16,128]{3,0,2,1:T(8,128)S(1)}, f32[32,2,16,128]{3,0,2,1:T(8,128)S(1)}, u32[]{:S(2)}, u32[]{:S(2)}) collective-permute-start(f32[32,2,16,128]{3,0,2,1:T(8,128)S(1)} %copy.76), channel_id=1, source_target_pairs={{32,0},{64,32},{96,64},{128,96},{160,128},{192,160},{224,192},{0,2... | collective-permute-start | bytes 1572872 | tf_op jit(solution)/shard_map/ppermute | solution.py:23
  19.0 15.3 %copy-start.4 = (f32[32,10,16,128]{3,0,2,1:T(8,128)}, f32[32,10,16,128]{3,0,2,1:T(8,128)S(1)}, u32[]{:S(2)}) copy-start(f32[32,10,16,128]{3,0,2,1:T(8,128)S(1)} %get-tuple-element.24) | copy-start | bytes 7864324
  20.7 13.6 %copy-start.3 = (f32[32,10,16,128]{3,0,2,1:T(8,128)}, f32[32,10,16,128]{3,0,2,1:T(8,128)S(1)}, u32[]{:S(2)}) copy-start(f32[32,10,16,128]{3,0,2,1:T(8,128)S(1)} %get-tuple-element.31) | copy-start | bytes 7864324
  20.7 13.6 %copy-start.2 = (f32[32,12,16,128]{3,0,2,1:T(8,128)}, f32[32,12,16,128]{3,0,2,1:T(8,128)S(1)}, u32[]{:S(2)}) copy-start(f32[32,12,16,128]{3,0,2,1:T(8,128)S(1)} %get-tuple-element.32) | copy-start | bytes 9437188
  20.8 13.5 %collective-permute-start.2 = (f32[32,12,2,128]{3,0,2,1:T(8,128)S(1)}, f32[32,12,2,128]{3,0,2,1:T(8,128)S(1)}, u32[]{:S(2)}, u32[]{:S(2)}) collective-permute-start(f32[32,12,2,128]{3,0,2,1:T(8,128)S(1)} %get-tuple-element.20), channel_id=1, source_target_pairs={{0,4},{4,8},{8,12},{12,16},{16,20},{20,24},{24,28},{28,0},{1,5},{5... | collective-permute-start | bytes 1179656 | tf_op jit(solution)/shard_map/ppermute | solution.py:22
  22.2 12.1 %collective-permute-start.3 = (f32[32,12,2,128]{3,0,2,1:T(8,128)S(1)}, f32[32,12,2,128]{3,0,2,1:T(8,128)S(1)}, u32[]{:S(2)}, u32[]{:S(2)}) collective-permute-start(f32[32,12,2,128]{3,0,2,1:T(8,128)S(1)} %get-tuple-element.21), channel_id=1, source_target_pairs={{4,0},{8,4},{12,8},{16,12},{20,16},{24,20},{28,24},{0,28},{5,1},{9... | collective-permute-start | bytes 1179656 | tf_op jit(solution)/shard_map/ppermute | solution.py:23
  42.8 8.1 %collective-permute-start.4 = (f32[32,12,20,2]{0,2,3,1:T(8,128)S(1)}, f32[32,12,20,2]{0,2,3,1:T(8,128)S(1)}, u32[]{:S(2)}, u32[]{:S(2)}) collective-permute-start(f32[32,12,20,2]{0,2,3,1:T(8,128)S(1)} %copy.44), channel_id=1, source_target_pairs={{0,1},{1,2},{2,3},{3,0},{4,5},{5,6},{6,7},{7,4},{8,9},{9,10},{10,1... | collective-permute-start | bytes 184328 | tf_op jit(solution)/shard_map/ppermute | solution.py:22
  47.6 6.7 %collective-permute-start.5 = (f32[32,12,20,2]{0,2,3,1:T(8,128)S(1)}, f32[32,12,20,2]{0,2,3,1:T(8,128)S(1)}, u32[]{:S(2)}, u32[]{:S(2)}) collective-permute-start(f32[32,12,20,2]{0,2,3,1:T(8,128)S(1)} %copy.47), channel_id=1, source_target_pairs={{1,0},{2,1},{3,2},{0,3},{5,4},{6,5},{7,6},{4,7},{9,8},{10,9},{11,1... | collective-permute-start | bytes 184328 | tf_op jit(solution)/shard_map/ppermute | solution.py:23
  53.8 3.3 %copy-start.6 = (f32[8,16,128]{2,1,0:T(8,128)S(1)}, f32[8,16,128]{2,1,0:T(8,128)}, u32[]{:S(2)}) copy-start(f32[8,16,128]{2,1,0:T(8,128)} %param.3) | copy-start | bytes 196612
  74.6 16.8 %copy-start.7 = (f32[8,16,128]{2,1,0:T(8,128)S(1)}, f32[8,16,128]{2,1,0:T(8,128)}, u32[]{:S(2)}) copy-start(f32[8,16,128]{2,1,0:T(8,128)} %param.3) | copy-start | bytes 196612
  74.6 11.5 %collective-permute-start.6 = (f32[32,2,16,128]{3,0,2,1:T(8,128)S(1)}, f32[32,2,16,128]{3,0,2,1:T(8,128)S(1)}, u32[]{:S(2)}, u32[]{:S(2)}) collective-permute-start(f32[32,2,16,128]{3,0,2,1:T(8,128)S(1)} %get-tuple-element.22), channel_id=1, source_target_pairs={{0,32},{32,64},{64,96},{96,128},{128,160},{160,192},{192,224},{224... | collective-permute-start | bytes 1572872 | tf_op jit(solution)/shard_map/ppermute | solution.py:22
  79.9 8.6 %collective-permute-start.7 = (f32[32,2,16,128]{3,0,2,1:T(8,128)S(1)}, f32[32,2,16,128]{3,0,2,1:T(8,128)S(1)}, u32[]{:S(2)}, u32[]{:S(2)}) collective-permute-start(f32[32,2,16,128]{3,0,2,1:T(8,128)S(1)} %get-tuple-element.23), channel_id=1, source_target_pairs={{32,0},{64,32},{96,64},{128,96},{160,128},{192,160},{224,192},{0,2... | collective-permute-start | bytes 1572872 | tf_op jit(solution)/shard_map/ppermute | solution.py:23
  88.6 11.5 %collective-permute-start.8 = (f32[32,12,2,128]{3,0,2,1:T(8,128)S(1)}, f32[32,12,2,128]{3,0,2,1:T(8,128)S(1)}, u32[]{:S(2)}, u32[]{:S(2)}) collective-permute-start(f32[32,12,2,128]{3,0,2,1:T(8,128)S(1)} %get-tuple-element.18), channel_id=1, source_target_pairs={{0,4},{4,8},{8,12},{12,16},{16,20},{20,24},{24,28},{28,0},{1,5},{5... | collective-permute-start | bytes 1179656 | tf_op jit(solution)/shard_map/ppermute | solution.py:22
  88.7 11.4 %collective-permute-start.9 = (f32[32,12,2,128]{3,0,2,1:T(8,128)S(1)}, f32[32,12,2,128]{3,0,2,1:T(8,128)S(1)}, u32[]{:S(2)}, u32[]{:S(2)}) collective-permute-start(f32[32,12,2,128]{3,0,2,1:T(8,128)S(1)} %get-tuple-element.19), channel_id=1, source_target_pairs={{4,0},{8,4},{12,8},{16,12},{20,16},{24,20},{28,24},{0,28},{5,1},{9... | collective-permute-start | bytes 1179656 | tf_op jit(solution)/shard_map/ppermute | solution.py:23
  100.1 0.8 copy-start.5
  113.7 16.2 %collective-permute-start.11 = (f32[32,12,20,2]{0,2,3,1:T(8,128)}, f32[32,12,20,2]{0,2,3,1:T(8,128)}, u32[]{:S(2)}, u32[]{:S(2)}) collective-permute-start(f32[32,12,20,2]{0,2,3,1:T(8,128)} %copy.53), channel_id=1, source_target_pairs={{1,0},{2,1},{3,2},{0,3},{5,4},{6,5},{7,6},{4,7},{9,8},{10,9},{11,1... | collective-permute-start | bytes 184328 | tf_op jit(solution)/shard_map/ppermute | solution.py:23
  116.3 9.8 %collective-permute-start.10 = (f32[32,12,20,2]{0,2,3,1:T(8,128)}, f32[32,12,20,2]{0,2,3,1:T(8,128)}, u32[]{:S(2)}, u32[]{:S(2)}) collective-permute-start(f32[32,12,20,2]{0,2,3,1:T(8,128)} %copy.51), channel_id=1, source_target_pairs={{0,1},{1,2},{2,3},{3,0},{4,5},{5,6},{6,7},{7,4},{8,9},{9,10},{10,1... | collective-permute-start | bytes 184328 | tf_op jit(solution)/shard_map/ppermute | solution.py:22
  143.9 1.3 copy-start
Sparse Core Ops, SparseCore 0:
  147.7 113.7 all-gather.2
